TPU v7x, 128 devices: a whole 4x4x4 slice. The times are simulated.
128 devices in a mesh: seq: 32 (over z, y, core), tp: 4 (over x).
Axes of the slice: x: 4, y: 4, z: 4, core: 2. Of those that a mesh axis runs over, the one named last changes fastest.
Arguments:
- tokens: bfloat16 [16384, 1408], P('seq'), may hold values from -70 to 70
- group_image: int32 [4096], P('seq'), may hold values from 0 to 31, never falling along the last dimension, each value on 1 to 512 neighbouring positions
- image_slot: int32 [32], replicated, may hold values from 0 to 31, each once
- attention_gain: float32 [1408], replicated, may hold values from 0.1 to 1.9
- query_weight: bfloat16 [1408, 1408], P(None, 'tp'), may hold values from -1.11930376 to 1.11930376
- key_weight: bfloat16 [1408, 1408], P(None, 'tp'), may hold values from -1.11930376 to 1.11930376
- value_weight: bfloat16 [1408, 1408], P(None, 'tp'), may hold values from -1.25 to 1.25
- output_weight: bfloat16 [1408, 1408], P('tp'), may hold values from -0.15625 to 0.15625
- feedforward_gain: float32 [1408], replicated, may hold values from 0.1 to 1.9
- up_weight: bfloat16 [1408, 6144], P(None, 'tp'), may hold values from -0.15625 to 0.15625
- down_weight: bfloat16 [6144, 1408], P('tp'), may hold values from -0.078125 to 0.078125
- merge_gain: float32 [1408], replicated, may hold values from 0.1 to 1.9
- merge_weight: bfloat16 [5632, 3584], P(None, 'tp'), may hold values from -0.078125 to 0.078125
Outputs:
- merged_rows: bfloat16 [32, 512, 3584], P('seq', None, 'tp')
Inputs may be any that keep to these rules, and one draw needn't show every extreme that they name: `group_image`: images are numbered in the order of their groups, each covers consecutive groups, 1 to 512 of them, and one covers exactly 512.
All inputs are finite; a program needn't handle non-finite values.
Results may differ from a plain program's by a relative error of at most 0.012.
Values may be sent and summed in bfloat16 or wider, within the bound.
No kernel may reach another device: no remote copies, remote signals or barrier semaphores. Data moves between devices by JAX's collectives and lax.ppermute only.
A program may use at most 192 MiB of HBM per device.

v0:
```python
import jax
import jax.numpy as jnp
from jax import lax
from jax.sharding import PartitionSpec as P

D = 1408
HD = 88
REACH = 4
epsilon = 1e-06
masked_score = -1e30


def shifted(value, axis, steps):
    count = lax.axis_size(axis)
    initial, last = (max(0, -steps), min(count, count - steps))
    return lax.ppermute(value, axis, [(source, source + steps) for source in range(initial, last)])


def finish_norm(hidden, row_mean, square, norm_gain):
    return (
        (hidden - row_mean) * lax.rsqrt(square - row_mean * row_mean + epsilon) * norm_gain
    ).astype(jnp.bfloat16)


def full_norm(hidden, norm_gain):
    row_mean = jnp.mean(hidden, axis=1, keepdims=True)
    square = jnp.mean(hidden * hidden, axis=1, keepdims=True)
    return finish_norm(hidden, row_mean, square, norm_gain)


def sum_rows(partial_value):
    return lax.psum(partial_value, "tp")


def attend_window(query_heads, key_heads, value_heads, query_image, key_image):
    scores = jnp.einsum(
        "qhd,khd->hqk", query_heads, key_heads, preferred_element_type=jnp.float32
    ) * HD ** (-0.5)
    same_image = query_image[:, None] == key_image[None, :]
    scores = jnp.where(same_image[None], scores, masked_score)
    row_best = jnp.max(scores, axis=2, keepdims=True)
    weights = jnp.exp(scores - row_best)
    row_total = jnp.sum(weights, axis=2)
    weighted = jnp.einsum(
        "hqk,khd->qhd",
        weights.astype(jnp.bfloat16),
        value_heads,
        preferred_element_type=jnp.float32,
    )
    return weighted / jnp.transpose(row_total)[:, :, None]


def shards(
    tokens,
    group_image,
    image_slot,
    attention_gain,
    query_weight,
    key_weight,
    value_weight,
    output_weight,
    feedforward_gain,
    up_weight,
    down_weight,
    merge_gain,
    merge_weight,
):
    device = lax.axis_index("seq")
    seq_count = lax.axis_size("seq")
    token_rows = tokens.shape[0]
    group_rows = group_image.shape[0]
    group_table = lax.all_gather(group_image, "seq", axis=0, tiled=True)
    token_image = jnp.repeat(group_table, 4)
    query_image = lax.dynamic_slice_in_dim(token_image, device * token_rows, token_rows, 0)
    residual = tokens.astype(jnp.float32)
    normed = full_norm(residual, attention_gain)
    head_count = query_weight.shape[1] // HD
    queries = jnp.dot(normed, query_weight, preferred_element_type=jnp.float32).astype(jnp.bfloat16)
    key_rows = jnp.dot(normed, key_weight, preferred_element_type=jnp.float32).astype(jnp.bfloat16)
    value_rows = jnp.dot(normed, value_weight, preferred_element_type=jnp.float32).astype(
        jnp.bfloat16
    )
    query_heads = queries.reshape(token_rows, head_count, HD)
    key_value = jnp.stack([key_rows, value_rows])
    arrived = []
    for offset in range(REACH, -REACH - 1, -1):
        if offset == 0:
            arrived.append(key_value)
        else:
            arrived.append(shifted(key_value, "seq", offset))
    window = jnp.concatenate(arrived, axis=1)
    reach_rows = REACH * token_rows
    image_pad = jnp.full((reach_rows,), -1, jnp.int32)
    image_padded = jnp.concatenate([image_pad, token_image, image_pad], axis=0)
    key_image = lax.dynamic_slice_in_dim(
        image_padded, device * token_rows, (2 * REACH + 1) * token_rows, 0
    )
    context = attend_window(
        query_heads,
        window[0].reshape(-1, head_count, HD),
        window[1].reshape(-1, head_count, HD),
        query_image,
        key_image,
    )
    context = context.astype(jnp.bfloat16).reshape(token_rows, head_count * HD)
    attention_part = jnp.dot(context, output_weight, preferred_element_type=jnp.float32)
    after_attention = residual + sum_rows(attention_part)
    normed_two = full_norm(after_attention, feedforward_gain)
    hidden_units = jax.nn.gelu(
        jnp.dot(normed_two, up_weight, preferred_element_type=jnp.float32), approximate=False
    ).astype(jnp.bfloat16)
    after_feedforward = after_attention + sum_rows(
        jnp.dot(hidden_units, down_weight, preferred_element_type=jnp.float32)
    )
    normed_three = full_norm(after_feedforward, merge_gain)
    grouped = normed_three.reshape(group_rows, 4 * D)
    projected = jnp.dot(grouped, merge_weight, preferred_element_type=jnp.float32).astype(
        jnp.bfloat16
    )
    image_count = image_slot.shape[0]
    image_ids = jnp.arange(image_count, dtype=jnp.int32)
    own_image = jnp.sum(jnp.where(image_slot == device, image_ids, 0))
    first_group = jnp.sum((group_table < own_image).astype(jnp.int32))
    group_count = jnp.sum((group_table == own_image).astype(jnp.int32))
    most_rows = REACH * group_rows
    row_numbers = jnp.arange(most_rows, dtype=jnp.int32)
    kept_rows = row_numbers < group_count
    out_cols = projected.shape[1]
    my_images = lax.dynamic_slice_in_dim(group_table, device * group_rows, group_rows, 0)
    target = jnp.sum(
        jnp.where(my_images[:, None] == image_ids[None, :], image_slot[None, :], 0), axis=1
    )
    owners = jnp.arange(seq_count, dtype=jnp.int32)
    outgoing = jnp.where(
        (target[None, :] == owners[:, None])[:, :, None],
        projected[None],
        jnp.zeros((), jnp.bfloat16),
    )
    received = lax.all_to_all(outgoing, "seq", split_axis=0, concat_axis=0, tiled=True).reshape(
        seq_count * group_rows, out_cols
    )
    padded = jnp.concatenate([received, jnp.zeros((most_rows, out_cols), jnp.bfloat16)], axis=0)
    own_block = lax.dynamic_slice_in_dim(padded, first_group, most_rows, 0)
    return jnp.where(kept_rows[:, None], own_block, jnp.zeros((), jnp.bfloat16))[None]


def solution(mesh):
    return jax.shard_map(
        shards,
        mesh=mesh,
        in_specs=(
            P("seq", None),
            P("seq"),
            P(),
            P(),
            P(None, "tp"),
            P(None, "tp"),
            P(None, "tp"),
            P("tp", None),
            P(),
            P(None, "tp"),
            P("tp", None),
            P(),
            P(None, "tp"),
        ),
        out_specs=P("seq", None, "tp"),
        check_vma=False,
    )
```

profile of v0, /device:TPU:0, one launch (start us, length us, event | category | flops | bytes accessed | tf_op | source)
XLA Modules:
  0.0 497.9 jit_solution(5010891190266689677)
XLA Ops:
  6.5 0.0 all-reduce.4.cloned.1.call-start
  6.5 2.0 convert_reduce_fusion
  8.6 1.9 fusion.18
  10.4 0.0 copy-done.9
  10.5 0.0 copy-start.10
  10.5 0.8 fusion.63
  11.2 1.0 copy-done.10
  12.2 0.8 fusion.62
  13.0 1.0 pad_maximum_fusion
  14.0 1.3 collective-permute-start.4
  15.2 3.9 collective-permute-start.3
  19.2 3.6 collective-permute-start.2
  22.7 3.9 collective-permute-start.1
  26.6 5.6 %collective-permute-start = (bf16[2,512,352]{1,2,0:T(8,128)(2,1)}, bf16[2,512,352]{1,2,0:T(8,128)(2,1)}, u32[]{:S(2)}, u32[]{:S(2)}) collective-permute-start(bf16[2,512,352]{1,2,0:T(8,128)(2,1)} %pad_maximum_fusion), channel_id=1, source_target_pairs={{0,16},{4,20},{8,24},{12,28},{16,32},{20,36},{24,40},{28,44},{32,4... | collective-permute-start | bytes 2162696 | tf_op jit(solution)/shard_map/ppermute | solution.py:16
  32.2 62.3 %all-gather = s32[32,1,128]{2,1,0:T(1,128)S(1)} all-gather(s32[1,1,128]{2,1,0:T(1,128)S(1)} %bitcast.42), channel_id=1, replica_groups=mesh['seq'=32,'tp'=4] {'seq'}, dimensions={0}, use_global_device_ids=true | all-gather | bytes 16896 | tf_op jit(solution)/shard_map/all_gather | solution.py:72
  94.5 0.6 broadcast_in_dim.97
  95.1 1.6 reshape.126
  96.8 0.1 dynamic_slice.13
  96.9 0.1 fusion.73
  97.0 1.3 broadcast_compare_fusion
  98.3 3.2 convolution_convert_fusion
  101.5 0.0 collective-permute-done
  101.5 1.4 collective-permute-start.5
  102.9 1.2 constant_dynamic-update-slice_fusion.8
  104.0 0.0 collective-permute-done.1
  104.1 1.3 collective-permute-start.6
  105.4 1.2 constant_dynamic-update-slice_fusion.7
  106.5 0.0 collective-permute-done.2
  106.5 1.5 collective-permute-start.7
  108.0 1.2 constant_dynamic-update-slice_fusion.6
  109.2 0.0 collective-permute-done.3
  109.2 1.2 constant_dynamic-update-slice_fusion.5
  110.4 0.0 collective-permute-done.4
  110.4 1.2 constant_dynamic-update-slice_fusion.3
  111.6 11.1 %collective-permute-done.5 = bf16[2,512,352]{1,2,0:T(8,128)(2,1)S(1)} collective-permute-done((bf16[2,512,352]{1,2,0:T(8,128)(2,1)}, bf16[2,512,352]{1,2,0:T(8,128)(2,1)S(1)}, u32[]{:S(2)}, u32[]{:S(2)}) %collective-permute-start.5) | collective-permute-done | bytes 720928 | tf_op jit(solution)/shard_map/ppermute | solution.py:16
  122.7 7.1 %collective-permute-done.6 = bf16[2,512,352]{1,2,0:T(8,128)(2,1)S(1)} collective-permute-done((bf16[2,512,352]{1,2,0:T(8,128)(2,1)}, bf16[2,512,352]{1,2,0:T(8,128)(2,1)S(1)}, u32[]{:S(2)}, u32[]{:S(2)}) %collective-permute-start.6) | collective-permute-done | bytes 720928 | tf_op jit(solution)/shard_map/ppermute | solution.py:16
  129.8 4.5 collective-permute-done.7
  134.4 3.1 fusion.109
  137.6 18.3 %fusion = (f32[4,512]{1,0:T(4,128)S(1)}, f32[4,512,4608]{2,1,0:T(8,128)}) fusion(pred[512,4608]{1,0:T(8,128)(4,1)S(1)} %broadcast_compare_fusion, bf16[512,4,88]{0,2,1:T(8,128)(2,1)S(1)} %bitcast.43, bf16[4608,4,88]{0,2,1:T(8,128)(2,1)} %bitcast.36), kind=kOutput, calls=%fused_computation.2 | convolution fusion | flops 1689253888 | bytes 43720704 | tf_op jit(solution)/shard_map/qhd,khd->hqk/dot_general | solution.py:36
  155.8 17.5 %fusion.1 = f32[4,512]{1,0:T(4,128)S(1)} fusion(f32[4,512,4608]{2,1,0:T(8,128)} %get-tuple-element.23, f32[4,512]{1,0:T(4,128)S(1)} %get-tuple-element.22, pred[512,4608]{1,0:T(8,128)(4,1)S(1)} %broadcast_compare_fusion), kind=kLoop, calls=%fused_computation.3 | loop fusion | flops 37746688 | bytes 40124416 | tf_op jit(solution)/shard_map/reduce_sum | solution.py:43
  173.3 15.3 %fusion.67 = bf16[512,4,88]{0,2,1:T(8,128)(2,1)S(1)} fusion(bf16[4608,4,88]{0,2,1:T(8,128)(2,1)S(1)} %bitcast.35, f32[4,512,4608]{2,1,0:T(8,128)} %get-tuple-element.23, f32[4,512]{1,0:T(4,128)S(1)} %get-tuple-element.22, pred[512,4608]{1,0:T(8,128)(4,1)S(1)} %broadcast_compare_fusion, f32[512,4]{0,1:T(4,128)S(1)} %bitcast.41), kind=kOutput, calls=%fused_computation.84 | convolution fusion | flops 1699053568 | bytes 43728896 | tf_op jit(solution)/shard_map/hqk,khd->qhd/dot_general | solution.py:44
  188.6 0.0 copy-start.2
  188.6 2.6 fusion.110
  191.2 0.0 all-reduce.4.cloned.1.call-update
  191.3 0.3 all-reduce.6.cloned.1.call-start
  191.5 90.3 %all-reduce.4.cloned.1.call-done = f32[512,1408]{1,0:T(8,128)} async-done(((f32[512,1408]{1,0:T(8,128)}), f32[512,1408]{1,0:T(8,128)}) %all-reduce.4.cloned.1.call-update) | async-done | bytes 2883600 | tf_op jit(solution)/shard_map/psum | solution.py:32
  281.8 2.5 fusion.71
  284.3 0.0 copy-start.12
  284.3 16.3 %fusion.20 = f32[512,1408]{1,0:T(8,128)} fusion(bf16[1536,1408]{1,0:T(8,128)(2,1)} %param.23, bf16[1408,1536]{1,0:T(8,128)(2,1)} %param.22, f32[1408]{0:T(1024)S(1)} %copy-done.11, f32[512]{0:T(512)S(1)} %get-tuple-element.19, f32[512]{0:T(512)S(1)} %get-tuple-element.18, f32[512,1408]{1,0:T(8,128)} %all-reduce.4.cloned.1.call-done, ...), kind=kOutput, calls=%fused_computation.41 | convolution fusion | flops 4484628480 | bytes 15869440 | tf_op jit(solution)/shard_map/dot_general | solution.py:113
  300.6 0.0 all-reduce.6.cloned.1.call-update
  300.6 0.1 dynamic_slice.12
  300.7 0.1 select_reduce_fusion
  300.8 71.2 %all-reduce.6.cloned.1.call-done = f32[512,1408]{1,0:T(8,128)} async-done(((f32[512,1408]{1,0:T(8,128)}), f32[512,1408]{1,0:T(8,128)}) %all-reduce.6.cloned.1.call-update) | async-done | bytes 2883600 | tf_op jit(solution)/shard_map/psum | solution.py:32
  372.0 3.4 fusion.107
  375.5 1.6 multiply_convert_fusion
  377.0 2.7 reshape.129
  379.7 5.5 %convolution_convert_fusion.3 = bf16[128,896]{1,0:T(8,128)(2,1)S(1)} fusion(bf16[128,5632]{1,0:T(8,128)(2,1)S(1)} %reshape.129, bf16[5632,896]{1,0:T(8,128)(2,1)} %param.25), kind=kOutput, calls=%fused_computation.82 | convolution fusion | flops 1291960320 | bytes 11763712 | tf_op jit(solution)/shard_map/dot_general | solution.py:117
  385.2 3.8 broadcast_select_fusion
  389.1 7.4 %all-to-all-start = ((bf16[32,128,896]{2,1,0:T(8,128)(2,1)}), bf16[32,128,896]{2,1,0:T(8,128)(2,1)}, u32[]{:S(2)}, u32[]{:S(2)}) async-start(bf16[32,128,896]{2,1,0:T(8,128)(2,1)} %broadcast_select_fusion), calls=%async_computation | async-start | bytes 14680064 | tf_op jit(solution)/shard_map/all_to_all | solution.py:139
  396.4 0.6 fusion.74
  397.1 1.4 convert_reduce_fusion.2
  400.5 0.6 iota_compare_fusion.2
  401.2 87.6 %all-to-all-done = bf16[32,128,896]{2,1,0:T(8,128)(2,1)} async-done(((bf16[32,128,896]{2,1,0:T(8,128)(2,1)}), bf16[32,128,896]{2,1,0:T(8,128)(2,1)}, u32[]{:S(2)}, u32[]{:S(2)}) %all-to-all-start) | async-done | bytes 7340064 | tf_op jit(solution)/shard_map/all_to_all | solution.py:139
  488.7 2.3 select_bitcast_fusion
  (32 shorter events, 0.3 us)
Async XLA Ops:
  6.5 182.1 %copy-start = (bf16[352,1408]{1,0:T(8,128)(2,1)S(1)}, bf16[352,1408]{1,0:T(8,128)(2,1)}, u32[]{:S(2)}) copy-start(bf16[352,1408]{1,0:T(8,128)(2,1)} %param.20) | copy-start | bytes 2973700
  6.5 3.9 copy-start.9
  6.5 275.3 %all-reduce.4.cloned.1.call-start = ((), (), s32[]{:S(2)}) async-start(), calls=%async_computation.1 | async-start | bytes 5767168 | tf_op jit(solution)/shard_map/psum | solution.py:32
  10.5 2.5 copy-start.4
  10.5 1.7 copy-start.10
  12.2 20.1 %copy-start.8 = (s32[128]{0:T(128)S(1)}, s32[128]{0:T(128)}, u32[]{:S(2)}) copy-start(s32[128]{0:T(128)} %param.14) | copy-start | bytes 1540
  13.0 1.0 copy-start.5
  14.0 96.5 %collective-permute-start.4 = (bf16[2,512,352]{1,2,0:T(8,128)(2,1)}, bf16[2,512,352]{1,2,0:T(8,128)(2,1)}, u32[]{:S(2)}, u32[]{:S(2)}) collective-permute-start(bf16[2,512,352]{1,2,0:T(8,128)(2,1)} %pad_maximum_fusion), channel_id=1, source_target_pairs={{4,0},{8,4},{12,8},{16,12},{20,16},{24,20},{28,24},{32,28},{36,32}... | collective-permute-start | bytes 2162696 | tf_op jit(solution)/shard_map/ppermute | solution.py:16
  15.2 93.9 %collective-permute-start.3 = (bf16[2,512,352]{1,2,0:T(8,128)(2,1)}, bf16[2,512,352]{1,2,0:T(8,128)(2,1)}, u32[]{:S(2)}, u32[]{:S(2)}) collective-permute-start(bf16[2,512,352]{1,2,0:T(8,128)(2,1)} %pad_maximum_fusion), channel_id=1, source_target_pairs={{0,4},{4,8},{8,12},{12,16},{16,20},{20,24},{24,28},{28,32},{32,36}... | collective-permute-start | bytes 2162696 | tf_op jit(solution)/shard_map/ppermute | solution.py:16
  19.2 87.4 %collective-permute-start.2 = (bf16[2,512,352]{1,2,0:T(8,128)(2,1)}, bf16[2,512,352]{1,2,0:T(8,128)(2,1)}, u32[]{:S(2)}, u32[]{:S(2)}) collective-permute-start(bf16[2,512,352]{1,2,0:T(8,128)(2,1)} %pad_maximum_fusion), channel_id=1, source_target_pairs={{0,8},{4,12},{8,16},{12,20},{16,24},{20,28},{24,32},{28,36},{32,40... | collective-permute-start | bytes 2162696 | tf_op jit(solution)/shard_map/ppermute | solution.py:16
  22.7 81.3 %collective-permute-start.1 = (bf16[2,512,352]{1,2,0:T(8,128)(2,1)}, bf16[2,512,352]{1,2,0:T(8,128)(2,1)}, u32[]{:S(2)}, u32[]{:S(2)}) collective-permute-start(bf16[2,512,352]{1,2,0:T(8,128)(2,1)} %pad_maximum_fusion), channel_id=1, source_target_pairs={{0,12},{4,16},{8,20},{12,24},{16,28},{20,32},{24,36},{28,40},{32,4... | collective-permute-start | bytes 2162696 | tf_op jit(solution)/shard_map/ppermute | solution.py:16
  26.6 74.9 %collective-permute-start = (bf16[2,512,352]{1,2,0:T(8,128)(2,1)}, bf16[2,512,352]{1,2,0:T(8,128)(2,1)}, u32[]{:S(2)}, u32[]{:S(2)}) collective-permute-start(bf16[2,512,352]{1,2,0:T(8,128)(2,1)} %pad_maximum_fusion), channel_id=1, source_target_pairs={{0,16},{4,20},{8,24},{12,28},{16,32},{20,36},{24,40},{28,44},{32,4... | collective-permute-start | bytes 2162696 | tf_op jit(solution)/shard_map/ppermute | solution.py:16
  101.5 8.9 %copy-start.6 = (bf16[1,512,352]{1,2,0:T(8,128)(2,1)S(1)}, bf16[1,512,352]{1,2,0:T(8,128)(2,1)}, u32[]{:S(2)}) copy-start(bf16[1,512,352]{1,2,0:T(8,128)(2,1)} %copy-done.5) | copy-start | bytes 1081348
  101.5 21.2 %collective-permute-start.5 = (bf16[2,512,352]{1,2,0:T(8,128)(2,1)}, bf16[2,512,352]{1,2,0:T(8,128)(2,1)S(1)}, u32[]{:S(2)}, u32[]{:S(2)}) collective-permute-start(bf16[2,512,352]{1,2,0:T(8,128)(2,1)} %pad_maximum_fusion), channel_id=1, source_target_pairs={{8,0},{12,4},{16,8},{20,12},{24,16},{28,20},{32,24},{36,28},{40,32... | collective-permute-start | bytes 2162696 | tf_op jit(solution)/shard_map/ppermute | solution.py:16
  104.1 25.7 %collective-permute-start.6 = (bf16[2,512,352]{1,2,0:T(8,128)(2,1)}, bf16[2,512,352]{1,2,0:T(8,128)(2,1)S(1)}, u32[]{:S(2)}, u32[]{:S(2)}) collective-permute-start(bf16[2,512,352]{1,2,0:T(8,128)(2,1)} %pad_maximum_fusion), channel_id=1, source_target_pairs={{12,0},{16,4},{20,8},{24,12},{28,16},{32,20},{36,24},{40,28},{44,3... | collective-permute-start | bytes 2162696 | tf_op jit(solution)/shard_map/ppermute | solution.py:16
  106.5 27.8 %collective-permute-start.7 = (bf16[2,512,352]{1,2,0:T(8,128)(2,1)}, bf16[2,512,352]{1,2,0:T(8,128)(2,1)S(1)}, u32[]{:S(2)}, u32[]{:S(2)}) collective-permute-start(bf16[2,512,352]{1,2,0:T(8,128)(2,1)} %pad_maximum_fusion), channel_id=1, source_target_pairs={{16,0},{20,4},{24,8},{28,12},{32,16},{36,20},{40,24},{44,28},{48,3... | collective-permute-start | bytes 2162696 | tf_op jit(solution)/shard_map/ppermute | solution.py:16
  134.4 3.2 copy-start.13
  155.8 17.5 %copy-start.3 = (bf16[1,4608,352]{1,2,0:T(8,128)(2,1)S(1)}, bf16[1,4608,352]{1,2,0:T(8,128)(2,1)}, u32[]{:S(2)}) copy-start(bf16[1,4608,352]{1,2,0:T(8,128)(2,1)} %get-tuple-element.15) | copy-start | bytes 9732100
  188.6 93.2 %copy-start.2 = (bf16[512,1408]{1,0:T(8,128)(2,1)S(1)}, bf16[512,1408]{1,0:T(8,128)(2,1)}, u32[]{:S(2)}) copy-start(bf16[512,1408]{1,0:T(8,128)(2,1)} %param.13) | copy-start | bytes 4325380
  191.2 93.1 %copy-start.11 = (f32[1408]{0:T(1024)S(1)}, f32[1408]{0:T(1024)}, u32[]{:S(2)}) copy-start(f32[1408]{0:T(1024)} %param.21) | copy-start | bytes 16900
  191.3 180.8 %all-reduce.6.cloned.1.call-start = ((), (), s32[]{:S(2)}) async-start(), calls=%async_computation.2 | async-start | bytes 5767168 | tf_op jit(solution)/shard_map/psum | solution.py:32
  284.3 16.4 %copy-start.12 = (s32[32]{0:T(128)S(1)}, s32[32]{0:T(128)}, u32[]{:S(2)}) copy-start(s32[32]{0:T(128)} %param.15) | copy-start | bytes 388
  300.8 74.7 %copy-start.7 = (f32[1408]{0:T(1024)S(1)}, f32[1408]{0:T(1024)}, u32[]{:S(2)}) copy-start(f32[1408]{0:T(1024)} %param.24) | copy-start | bytes 16900
  389.1 99.7 %all-to-all-start = ((bf16[32,128,896]{2,1,0:T(8,128)(2,1)}), bf16[32,128,896]{2,1,0:T(8,128)(2,1)}, u32[]{:S(2)}, u32[]{:S(2)}) async-start(bf16[32,128,896]{2,1,0:T(8,128)(2,1)} %broadcast_select_fusion), calls=%async_computation | async-start | bytes 14680064 | tf_op jit(solution)/shard_map/all_to_all | solution.py:139
  488.7 2.3 copy-start.1
Sparse Core Ops, SparseCore 0:
  191.4 90.3 all-reduce.3
  300.7 71.2 all-reduce.5
where the time goes:
time: 499 us; the launch traced here: 498 us
  waiting for transfers between devices  272 us (55%)
  matrix products  62.6 us (13%)
  blocking collectives  62.3 us (12%)
  other arithmetic  40.1 us (8%)
  starting transfers between devices  30.1 us (6%)
  between operations  15.8 us (3%)
  local copies, waits for them, and re-layouts  15.2 us (3%)
    psum x2, waiting for transfers between devices, sum_rows(): return lax.psum(partial_value, 'tp')  162 us
    all_to_all x1, waiting for transfers between devices, shards(): lax.all_to_all(outgoing, 'seq', split_axis=0, concat_axis=0, tiled=True)  87.6 us
    all_gather x1, blocking collectives, shards(): group_table = lax.all_gather(group_image, 'seq', axis=0, tiled=True)  62.3 us
    ppermute x8, waiting for transfers between devices, shifted(): lax.ppermute(value, axis, [(source, source + steps) for source in range(i...  22.7 us
    ppermute x8, starting transfers between devices, shifted(): lax.ppermute(value, axis, [(source, source + steps) for source in range(i...  22.5 us
    dot_general x1, matrix products, attend_window(): jnp.einsum('qhd,khd->hqk', query_heads, key_heads, preferred_element_type...  18.3 us
    reduce_sum x1, other arithmetic, attend_window(): row_total = jnp.sum(weights, axis=2)  17.5 us
    dot_general x1, matrix products, shards(): jnp.dot(hidden_units, down_weight, preferred_element_type=jnp.float32)  16.3 us
  transfers between devices with their start and end apart: 11, of which 6 were waited for; matrix products, arithmetic and copies ran while one was open for 3% of the time, Pallas kernels for 0%

commit v1 on v0

--- a/solution.py
+++ b/solution.py
@@ -29,7 +29,12 @@
 
 
 def sum_rows(partial_value):
-    return lax.psum(partial_value, "tp")
+
+    def shelves_begin(t0):
+        then = lax.all_gather(t0, "tp").sum(axis=0)
+        return then
+
+    return shelves_begin(partial_value)
 
 
 def attend_window(query_heads, key_heads, value_heads, query_image, key_image):

time: 499 us -> 591 us (1.18)
  waiting for transfers between devices: 272 us -> 350 us
  other arithmetic: 40.1 us -> 54.1 us
    all_gather x0 -> x2, waiting for transfers between devices: none -> 239 us  [shelves_begin(): then = lax.all_gather(t0, 'tp').sum(axis=0)]
    psum x2 -> x0, waiting for transfers between devices: 162 us -> none  [sum_rows(): return lax.psum(partial_value, 'tp')]
    reduce_sum x0 -> x2, other arithmetic: none -> 14 us  [shelves_begin(): then = lax.all_gather(t0, 'tp').sum(axis=0)]
where the time goes in v1:
time: 591 us; the launch traced here: 590 us
  waiting for transfers between devices  350 us (59%)
  matrix products  62.6 us (11%)
  blocking collectives  62.3 us (11%)
  other arithmetic  54.1 us (9%)
  starting transfers between devices  30.1 us (5%)
  between operations  15.8 us (3%)
  local copies, waits for them, and re-layouts  15.1 us (3%)
    all_gather x2, waiting for transfers between devices, shelves_begin(): then = lax.all_gather(t0, 'tp').sum(axis=0)  239 us
    all_to_all x1, waiting for transfers between devices, shards(): lax.all_to_all(outgoing, 'seq', split_axis=0, concat_axis=0, tiled=True)  87.6 us
    all_gather x1, blocking collectives, shards(): group_table = lax.all_gather(group_image, 'seq', axis=0, tiled=True)  62.3 us
    ppermute x8, waiting for transfers between devices, shifted(): lax.ppermute(value, axis, [(source, source + steps) for source in range(i...  22.7 us
    ppermute x8, starting transfers between devices, shifted(): lax.ppermute(value, axis, [(source, source + steps) for source in range(i...  22.5 us
    dot_general x1, matrix products, attend_window(): jnp.einsum('qhd,khd->hqk', query_heads, key_heads, preferred_element_type...  18.3 us
    reduce_sum x1, other arithmetic, attend_window(): row_total = jnp.sum(weights, axis=2)  17.5 us
    dot_general x1, matrix products, shards(): jnp.dot(hidden_units, down_weight, preferred_element_type=jnp.float32)  16.2 us
  transfers between devices with their start and end apart: 11, of which 6 were waited for; matrix products, arithmetic and copies ran while one was open for 3% of the time, Pallas kernels for 0%

profile of v1, /device:TPU:0, one launch (start us, length us, event | category | flops | bytes accessed | tf_op | source)
XLA Modules:
  0.0 589.6 jit_solution(12941045562943322514)
XLA Ops:
  6.5 0.0 all-gather.6.cloned.1.call-start
  6.5 2.0 convert_reduce_fusion
  8.6 1.9 fusion.18
  10.5 0.0 copy-start.10
  10.5 0.8 fusion.63
  11.2 1.0 copy-done.10
  12.2 0.8 fusion.62
  13.0 1.0 pad_maximum_fusion
  14.0 1.3 collective-permute-start.4
  15.2 3.9 collective-permute-start.3
  19.2 3.6 collective-permute-start.2
  22.7 3.9 collective-permute-start.1
  26.6 5.6 collective-permute-start
  32.2 62.3 %all-gather.2 = s32[32,1,128]{2,1,0:T(1,128)S(1)} all-gather(s32[1,1,128]{2,1,0:T(1,128)S(1)} %bitcast.46), channel_id=1, replica_groups=mesh['seq'=32,'tp'=4] {'seq'}, dimensions={0}, use_global_device_ids=true | all-gather | bytes 16896 | tf_op jit(solution)/shard_map/all_gather | solution.py:77
  94.5 0.6 broadcast_in_dim.97
  95.1 1.6 reshape.126
  96.8 0.1 dynamic_slice.13
  96.9 0.1 fusion.73
  97.0 1.3 broadcast_compare_fusion
  98.3 3.2 convolution_convert_fusion
  101.5 0.0 collective-permute-done
  101.5 1.4 collective-permute-start.5
  102.9 1.2 constant_dynamic-update-slice_fusion.8
  104.0 0.0 collective-permute-done.1
  104.1 1.3 collective-permute-start.6
  105.4 1.2 constant_dynamic-update-slice_fusion.7
  106.5 0.0 collective-permute-done.2
  106.5 1.5 collective-permute-start.7
  108.0 1.2 constant_dynamic-update-slice_fusion.6
  109.2 0.0 collective-permute-done.3
  109.2 1.2 constant_dynamic-update-slice_fusion.5
  110.4 0.0 collective-permute-done.4
  110.4 1.2 constant_dynamic-update-slice_fusion.3
  111.6 11.1 %collective-permute-done.5 = bf16[2,512,352]{1,2,0:T(8,128)(2,1)S(1)} collective-permute-done((bf16[2,512,352]{1,2,0:T(8,128)(2,1)}, bf16[2,512,352]{1,2,0:T(8,128)(2,1)S(1)}, u32[]{:S(2)}, u32[]{:S(2)}) %collective-permute-start.5) | collective-permute-done | bytes 720928 | tf_op jit(solution)/shard_map/ppermute | solution.py:16
  122.7 7.1 %collective-permute-done.6 = bf16[2,512,352]{1,2,0:T(8,128)(2,1)S(1)} collective-permute-done((bf16[2,512,352]{1,2,0:T(8,128)(2,1)}, bf16[2,512,352]{1,2,0:T(8,128)(2,1)S(1)}, u32[]{:S(2)}, u32[]{:S(2)}) %collective-permute-start.6) | collective-permute-done | bytes 720928 | tf_op jit(solution)/shard_map/ppermute | solution.py:16
  129.8 4.5 collective-permute-done.7
  134.4 3.1 fusion.109
  137.6 18.3 %fusion = (f32[4,512]{1,0:T(4,128)S(1)}, f32[4,512,4608]{2,1,0:T(8,128)}) fusion(pred[512,4608]{1,0:T(8,128)(4,1)S(1)} %broadcast_compare_fusion, bf16[512,4,88]{0,2,1:T(8,128)(2,1)S(1)} %bitcast.47, bf16[4608,4,88]{0,2,1:T(8,128)(2,1)} %bitcast.40), kind=kOutput, calls=%fused_computation.2 | convolution fusion | flops 1689253888 | bytes 43720704 | tf_op jit(solution)/shard_map/qhd,khd->hqk/dot_general | solution.py:41
  155.8 17.5 %fusion.1 = f32[4,512]{1,0:T(4,128)S(1)} fusion(f32[4,512,4608]{2,1,0:T(8,128)} %get-tuple-element.23, f32[4,512]{1,0:T(4,128)S(1)} %get-tuple-element.22, pred[512,4608]{1,0:T(8,128)(4,1)S(1)} %broadcast_compare_fusion), kind=kLoop, calls=%fused_computation.3 | loop fusion | flops 37746688 | bytes 40124416 | tf_op jit(solution)/shard_map/reduce_sum | solution.py:48
  173.3 15.3 %fusion.67 = bf16[512,4,88]{0,2,1:T(8,128)(2,1)S(1)} fusion(bf16[4608,4,88]{0,2,1:T(8,128)(2,1)S(1)} %bitcast.39, f32[4,512,4608]{2,1,0:T(8,128)} %get-tuple-element.23, f32[4,512]{1,0:T(4,128)S(1)} %get-tuple-element.22, pred[512,4608]{1,0:T(8,128)(4,1)S(1)} %broadcast_compare_fusion, f32[512,4]{0,1:T(4,128)S(1)} %bitcast.45), kind=kOutput, calls=%fused_computation.84 | convolution fusion | flops 1699053568 | bytes 43728896 | tf_op jit(solution)/shard_map/hqk,khd->qhd/dot_general | solution.py:49
  188.6 2.7 fusion.110
  191.3 0.0 all-gather.6.cloned.1.call-update
  191.3 0.3 all-gather.8.cloned.1.call-start
  191.6 128.6 %all-gather.6.cloned.1.call-done = f32[2048,1408]{1,0:T(8,128)} async-done(((f32[512,1408]{1,0:T(8,128)}), f32[2048,1408]{1,0:T(8,128)}) %all-gather.6.cloned.1.call-update) | async-done | bytes 11534352 | tf_op jit(solution)/shard_map/all_gather | solution.py:34
  320.1 7.0 %reduce_sum.123 = f32[512,1408]{1,0:T(8,128)} reduce(f32[4,512,1408]{2,1,0:T(8,128)} %bitcast.38, f32[]{:T(128)} %constant.11.clone.1), dimensions={0}, to_apply=%region_7.8 | reduce | flops 2162688 | bytes 14417924 | tf_op jit(solution)/shard_map/reduce_sum | solution.py:34
  327.1 2.5 fusion.71
  329.6 0.0 copy-start.12
  329.6 16.2 %fusion.20 = f32[512,1408]{1,0:T(8,128)} fusion(bf16[1536,1408]{1,0:T(8,128)(2,1)} %param.23, bf16[1408,1536]{1,0:T(8,128)(2,1)} %param.22, f32[1408]{0:T(1024)S(1)} %copy-done.11, f32[512]{0:T(512)S(1)} %get-tuple-element.19, f32[512]{0:T(512)S(1)} %get-tuple-element.18, f32[512,1408]{1,0:T(8,128)} %reduce_sum.123, bf16[512,1408]{1,0:T(8,128)(2,1)S(1)} %copy-done.2), kind=kOutput, calls=%fused_computation.41 | convolution fusion | flops 4484628480 | bytes 15869440 | tf_op jit(solution)/shard_map/dot_general | solution.py:118
  345.8 0.0 all-gather.8.cloned.1.call-update
  345.9 0.1 dynamic_slice.12
  345.9 0.1 select_reduce_fusion
  346.0 110.7 %all-gather.8.cloned.1.call-done = f32[2048,1408]{1,0:T(8,128)} async-done(((f32[512,1408]{1,0:T(8,128)}), f32[2048,1408]{1,0:T(8,128)}) %all-gather.8.cloned.1.call-update) | async-done | bytes 11534352 | tf_op jit(solution)/shard_map/all_gather | solution.py:34
  456.7 7.0 %reduce_sum.126 = f32[512,1408]{1,0:T(8,128)} reduce(f32[4,512,1408]{2,1,0:T(8,128)} %bitcast.37, f32[]{:T(128)} %constant.11.clone.1), dimensions={0}, to_apply=%region_10.11 | reduce | flops 2162688 | bytes 14417924 | tf_op jit(solution)/shard_map/reduce_sum | solution.py:34
  463.7 3.4 fusion.107
  467.2 1.6 multiply_convert_fusion
  468.7 2.7 reshape.129
  471.4 5.5 convolution_convert_fusion.3
  477.0 3.8 broadcast_select_fusion
  480.8 7.4 %all-to-all-start = ((bf16[32,128,896]{2,1,0:T(8,128)(2,1)}), bf16[32,128,896]{2,1,0:T(8,128)(2,1)}, u32[]{:S(2)}, u32[]{:S(2)}) async-start(bf16[32,128,896]{2,1,0:T(8,128)(2,1)} %broadcast_select_fusion), calls=%async_computation | async-start | bytes 14680064 | tf_op jit(solution)/shard_map/all_to_all | solution.py:144
  488.2 0.6 fusion.74
  488.8 1.4 convert_reduce_fusion.2
  492.3 0.6 iota_compare_fusion.2
  492.9 87.6 %all-to-all-done = bf16[32,128,896]{2,1,0:T(8,128)(2,1)} async-done(((bf16[32,128,896]{2,1,0:T(8,128)(2,1)}), bf16[32,128,896]{2,1,0:T(8,128)(2,1)}, u32[]{:S(2)}, u32[]{:S(2)}) %all-to-all-start) | async-done | bytes 7340064 | tf_op jit(solution)/shard_map/all_to_all | solution.py:144
  580.5 2.3 select_bitcast_fusion
  (34 shorter events, 0.3 us)
Async XLA Ops:
  6.5 182.1 %copy-start = (bf16[352,1408]{1,0:T(8,128)(2,1)S(1)}, bf16[352,1408]{1,0:T(8,128)(2,1)}, u32[]{:S(2)}) copy-start(bf16[352,1408]{1,0:T(8,128)(2,1)} %param.20) | copy-start | bytes 2973700
  6.5 3.9 copy-start.9
  6.5 313.6 %all-gather.6.cloned.1.call-start = ((), (), s32[]{:S(2)}) async-start(), calls=%async_computation.1 | async-start | bytes 14417920 | tf_op jit(solution)/shard_map/all_gather | solution.py:34
  10.5 2.5 copy-start.4
  10.5 1.7 copy-start.10
  12.2 20.1 %copy-start.8 = (s32[128]{0:T(128)S(1)}, s32[128]{0:T(128)}, u32[]{:S(2)}) copy-start(s32[128]{0:T(128)} %param.14) | copy-start | bytes 1540
  13.0 1.0 copy-start.5
  14.0 96.5 %collective-permute-start.4 = (bf16[2,512,352]{1,2,0:T(8,128)(2,1)}, bf16[2,512,352]{1,2,0:T(8,128)(2,1)}, u32[]{:S(2)}, u32[]{:S(2)}) collective-permute-start(bf16[2,512,352]{1,2,0:T(8,128)(2,1)} %pad_maximum_fusion), channel_id=1, source_target_pairs={{4,0},{8,4},{12,8},{16,12},{20,16},{24,20},{28,24},{32,28},{36,32}... | collective-permute-start | bytes 2162696 | tf_op jit(solution)/shard_map/ppermute | solution.py:16
  15.2 93.9 %collective-permute-start.3 = (bf16[2,512,352]{1,2,0:T(8,128)(2,1)}, bf16[2,512,352]{1,2,0:T(8,128)(2,1)}, u32[]{:S(2)}, u32[]{:S(2)}) collective-permute-start(bf16[2,512,352]{1,2,0:T(8,128)(2,1)} %pad_maximum_fusion), channel_id=1, source_target_pairs={{0,4},{4,8},{8,12},{12,16},{16,20},{20,24},{24,28},{28,32},{32,36}... | collective-permute-start | bytes 2162696 | tf_op jit(solution)/shard_map/ppermute | solution.py:16
  19.2 87.4 %collective-permute-start.2 = (bf16[2,512,352]{1,2,0:T(8,128)(2,1)}, bf16[2,512,352]{1,2,0:T(8,128)(2,1)}, u32[]{:S(2)}, u32[]{:S(2)}) collective-permute-start(bf16[2,512,352]{1,2,0:T(8,128)(2,1)} %pad_maximum_fusion), channel_id=1, source_target_pairs={{0,8},{4,12},{8,16},{12,20},{16,24},{20,28},{24,32},{28,36},{32,40... | collective-permute-start | bytes 2162696 | tf_op jit(solution)/shard_map/ppermute | solution.py:16
  22.7 81.3 %collective-permute-start.1 = (bf16[2,512,352]{1,2,0:T(8,128)(2,1)}, bf16[2,512,352]{1,2,0:T(8,128)(2,1)}, u32[]{:S(2)}, u32[]{:S(2)}) collective-permute-start(bf16[2,512,352]{1,2,0:T(8,128)(2,1)} %pad_maximum_fusion), channel_id=1, source_target_pairs={{0,12},{4,16},{8,20},{12,24},{16,28},{20,32},{24,36},{28,40},{32,4... | collective-permute-start | bytes 2162696 | tf_op jit(solution)/shard_map/ppermute | solution.py:16
  26.6 74.9 %collective-permute-start = (bf16[2,512,352]{1,2,0:T(8,128)(2,1)}, bf16[2,512,352]{1,2,0:T(8,128)(2,1)}, u32[]{:S(2)}, u32[]{:S(2)}) collective-permute-start(bf16[2,512,352]{1,2,0:T(8,128)(2,1)} %pad_maximum_fusion), channel_id=1, source_target_pairs={{0,16},{4,20},{8,24},{12,28},{16,32},{20,36},{24,40},{28,44},{32,4... | collective-permute-start | bytes 2162696 | tf_op jit(solution)/shard_map/ppermute | solution.py:16
  101.5 8.9 %copy-start.6 = (bf16[1,512,352]{1,2,0:T(8,128)(2,1)S(1)}, bf16[1,512,352]{1,2,0:T(8,128)(2,1)}, u32[]{:S(2)}) copy-start(bf16[1,512,352]{1,2,0:T(8,128)(2,1)} %copy-done.5) | copy-start | bytes 1081348
  101.5 21.2 %collective-permute-start.5 = (bf16[2,512,352]{1,2,0:T(8,128)(2,1)}, bf16[2,512,352]{1,2,0:T(8,128)(2,1)S(1)}, u32[]{:S(2)}, u32[]{:S(2)}) collective-permute-start(bf16[2,512,352]{1,2,0:T(8,128)(2,1)} %pad_maximum_fusion), channel_id=1, source_target_pairs={{8,0},{12,4},{16,8},{20,12},{24,16},{28,20},{32,24},{36,28},{40,32... | collective-permute-start | bytes 2162696 | tf_op jit(solution)/shard_map/ppermute | solution.py:16
  104.1 25.7 %collective-permute-start.6 = (bf16[2,512,352]{1,2,0:T(8,128)(2,1)}, bf16[2,512,352]{1,2,0:T(8,128)(2,1)S(1)}, u32[]{:S(2)}, u32[]{:S(2)}) collective-permute-start(bf16[2,512,352]{1,2,0:T(8,128)(2,1)} %pad_maximum_fusion), channel_id=1, source_target_pairs={{12,0},{16,4},{20,8},{24,12},{28,16},{32,20},{36,24},{40,28},{44,3... | collective-permute-start | bytes 2162696 | tf_op jit(solution)/shard_map/ppermute | solution.py:16
  106.5 27.8 %collective-permute-start.7 = (bf16[2,512,352]{1,2,0:T(8,128)(2,1)}, bf16[2,512,352]{1,2,0:T(8,128)(2,1)S(1)}, u32[]{:S(2)}, u32[]{:S(2)}) collective-permute-start(bf16[2,512,352]{1,2,0:T(8,128)(2,1)} %pad_maximum_fusion), channel_id=1, source_target_pairs={{16,0},{20,4},{24,8},{28,12},{32,16},{36,20},{40,24},{44,28},{48,3... | collective-permute-start | bytes 2162696 | tf_op jit(solution)/shard_map/ppermute | solution.py:16
  134.4 3.2 copy-start.13
  155.8 17.5 %copy-start.3 = (bf16[1,4608,352]{1,2,0:T(8,128)(2,1)S(1)}, bf16[1,4608,352]{1,2,0:T(8,128)(2,1)}, u32[]{:S(2)}) copy-start(bf16[1,4608,352]{1,2,0:T(8,128)(2,1)} %get-tuple-element.15) | copy-start | bytes 9732100
  191.3 265.4 %all-gather.8.cloned.1.call-start = ((), (), s32[]{:S(2)}) async-start(), calls=%async_computation.2 | async-start | bytes 14417920 | tf_op jit(solution)/shard_map/all_gather | solution.py:34
  320.1 7.0 %copy-start.2 = (bf16[512,1408]{1,0:T(8,128)(2,1)S(1)}, bf16[512,1408]{1,0:T(8,128)(2,1)}, u32[]{:S(2)}) copy-start(bf16[512,1408]{1,0:T(8,128)(2,1)} %param.13) | copy-start | bytes 4325380
  327.1 2.5 copy-start.11
  329.6 16.4 %copy-start.12 = (s32[32]{0:T(128)S(1)}, s32[32]{0:T(128)}, u32[]{:S(2)}) copy-start(s32[32]{0:T(128)} %param.15) | copy-start | bytes 388
  463.7 3.4 copy-start.7
  480.8 99.7 %all-to-all-start = ((bf16[32,128,896]{2,1,0:T(8,128)(2,1)}), bf16[32,128,896]{2,1,0:T(8,128)(2,1)}, u32[]{:S(2)}, u32[]{:S(2)}) async-start(bf16[32,128,896]{2,1,0:T(8,128)(2,1)} %broadcast_select_fusion), calls=%async_computation | async-start | bytes 14680064 | tf_op jit(solution)/shard_map/all_to_all | solution.py:144
  580.5 2.3 copy-start.1
Sparse Core Ops, SparseCore 0:
  191.4 128.6 all-gather.5
  346.0 110.6 all-gather.7
